TPU v7x, 32 devices: a whole 2x2x4 slice. The times are simulated.
32 devices in a mesh: ep: 8 (over z, x), tp: 4 (over y, core).
Axes of the slice: x: 2, y: 2, z: 4, core: 2. Of those that a mesh axis runs over, the one named last changes fastest.
Arguments:
- features: bfloat16 [2048, 1024], P('ep'), may hold values from -6 to 6
- cotangent: bfloat16 [2048, 2048], P('ep'), may hold values from -6 to 6
- expert_ids: int32 [2048, 2], P('ep'), may hold values from 0 to 7, all different within a row; in each aligned block of 256 rows (0 to 255, 256 to 511, ...) at most 96 rows name the same one
- gate_levels: int32 [2048, 2], P('ep'), may hold values from 1 to 15
- w_in: bfloat16 [8, 1024, 4096], P('ep', None, 'tp'), may hold values from -0.1875 to 0.1875
- w_out: bfloat16 [8, 4096, 2048], P('ep', 'tp'), may hold values from -0.09375 to 0.09375
Outputs:
- grad_in: bfloat16 [2048, 1024], P('ep', 'tp')
- grad_w_in: bfloat16 [8, 1024, 4096], P('ep', None, 'tp')
- grad_w_out: bfloat16 [8, 4096, 2048], P('ep', 'tp')
Inputs may be any that keep to these rules, and one draw needn't show every extreme that they name: `expert_ids`: each row names two different experts. In each aligned block of 256 rows no expert is named by more than 96 rows, and some expert reaches 96 rows in some block.
All inputs are finite; a program needn't handle non-finite values.
Results may differ from a plain program's by a relative error of at most 0.0065.
Values may be sent and summed in bfloat16 or wider, within the bound.
No kernel may reach another device: no remote copies, remote signals or barrier semaphores. Data moves between devices by JAX's collectives and lax.ppermute only.
A program may use at most 128 MiB of HBM per device.

v0:
```python
import math
import jax
import jax.numpy as jnp
from jax import lax
from jax.sharding import PartitionSpec as P

E = 8


def shifted(value, axis, by):
    peers = lax.axis_size(axis)
    return lax.ppermute(value, axis, [(i, (i + by) % peers) for i in range(peers)])


def slot_positions(expert_ids, blocks, experts, capacity):
    flattened = expert_ids.reshape(blocks, -1)
    one_hot = (flattened[:, :, None] == jnp.arange(experts, dtype=jnp.int32)[None, None, :]).astype(
        jnp.int32
    )
    earlier = jnp.cumsum(one_hot, axis=1) - one_hot
    within = jnp.sum(one_hot * earlier, axis=2)
    block_ids = jnp.arange(blocks, dtype=jnp.int32)[:, None]
    return ((block_ids * experts + flattened) * capacity + within).reshape(-1)


def shards(features, cotangent, expert_ids, gate_levels, w_in, w_out):
    device_count = lax.axis_size("ep")
    replicas = device_count // E
    replica = lax.axis_index("ep") // E
    tokens_here = expert_ids.shape[0]
    sub_rows = tokens_here // replicas
    capacity = 3 * sub_rows // 8
    slot_count = device_count * capacity
    pair_count = 2 * tokens_here
    positions = slot_positions(expert_ids, replicas, E, capacity)
    owner = (
        jnp.full((slot_count,), pair_count, jnp.int32)
        .at[positions]
        .set(jnp.arange(pair_count, dtype=jnp.int32))
    )
    filled = owner < pair_count
    pair_ids = jnp.minimum(owner, pair_count - 1)
    token_ids = pair_ids // 2
    gate_values = gate_levels.reshape(-1).astype(jnp.float32) / 16.0
    slot_gates = jnp.where(filled, gate_values[pair_ids], 0.0)
    slot_mask = filled.astype(jnp.bfloat16)[:, None]
    packed_x = features[token_ids] * slot_mask
    packed_dy = (cotangent[token_ids].astype(jnp.float32) * slot_gates[:, None]).astype(
        jnp.bfloat16
    )
    rows_x, rows_dy = (
        lax.all_to_all(packed_x, "ep", split_axis=0, concat_axis=0, tiled=True),
        lax.all_to_all(packed_dy, "ep", split_axis=0, concat_axis=0, tiled=True),
    )
    piece_in = w_in[0]
    piece_out = w_out[0]
    span = piece_in.shape[1]
    weight_in = jnp.zeros((piece_in.shape[0], span * replicas), jnp.bfloat16)
    weight_out = jnp.zeros((span * replicas, piece_out.shape[1]), jnp.bfloat16)
    weight_in = lax.dynamic_update_slice_in_dim(weight_in, piece_in, replica * span, 1)
    weight_out = lax.dynamic_update_slice_in_dim(weight_out, piece_out, replica * span, 0)
    moving = (piece_in, piece_out)
    for turn_index in range(1, replicas):
        moving = shifted((moving[0], moving[1]), "ep", E)
        anchor = (replica - turn_index) % replicas
        weight_in = lax.dynamic_update_slice_in_dim(weight_in, moving[0], anchor * span, 1)
        weight_out = lax.dynamic_update_slice_in_dim(weight_out, moving[1], anchor * span, 0)
    pre = jnp.dot(rows_x, weight_in, preferred_element_type=jnp.float32)
    activated, gelu_back = jax.vjp(jax.nn.gelu, pre)
    act_rows = activated.astype(jnp.bfloat16)
    back_act = lax.dot_general(
        rows_dy, weight_out, (((1,), (1,)), ((), ())), preferred_element_type=jnp.float32
    )
    back_pre = gelu_back(back_act)[0].astype(jnp.bfloat16)
    summed = lax.psum_scatter(
        lax.dot_general(
            weight_in, back_pre, (((1,), (1,)), ((), ())), preferred_element_type=jnp.float32
        ),
        "tp",
        scatter_dimension=0,
        tiled=True,
    )
    returned = lax.all_to_all(
        summed.astype(jnp.bfloat16), "ep", split_axis=1, concat_axis=1, tiled=True
    )
    picked = returned[:, positions].astype(jnp.float32)
    grad_in = jnp.sum(picked.reshape(picked.shape[0], tokens_here, 2), axis=2).T.astype(
        jnp.bfloat16
    )

    def span_grads(first_span, span_total):
        width = span_total * span
        act_cols = lax.dynamic_slice_in_dim(act_rows, first_span * span, width, 1)
        pre_cols = lax.dynamic_slice_in_dim(back_pre, first_span * span, width, 1)
        grad_first = lax.dot_general(
            pre_cols, rows_x, (((0,), (0,)), ((), ())), preferred_element_type=jnp.float32
        )
        grad_second = lax.dot_general(
            act_cols, rows_dy, (((0,), (0,)), ((), ())), preferred_element_type=jnp.float32
        )
        return (grad_first, grad_second)

    summed_grads = span_grads((replica - 1) % replicas, 1)
    for turn_index in range(1, replicas):
        summed_grads = shifted((summed_grads[0], summed_grads[1]), "ep", E)
        own_grads = span_grads((replica - turn_index - 1) % replicas, 1)
        summed_grads = (summed_grads[0] + own_grads[0], summed_grads[1] + own_grads[1])
    grad_scale = 1.0 / math.sqrt(2.0 * tokens_here * device_count / E)
    grad_w_in = (summed_grads[0] * grad_scale).T.astype(jnp.bfloat16)[None]
    grad_w_out = (summed_grads[1] * grad_scale).astype(jnp.bfloat16)[None]
    return (grad_in, grad_w_in, grad_w_out)


def solution(mesh):
    return jax.shard_map(
        shards,
        mesh=mesh,
        in_specs=(
            P("ep", None),
            P("ep", None),
            P("ep", None),
            P("ep", None),
            P("ep", None, "tp"),
            P("ep", "tp", None),
        ),
        out_specs=(P("ep", "tp"), P("ep", None, "tp"), P("ep", "tp", None)),
        check_vma=False,
    )
```

profile of v0, /device:TPU:0, one launch (start us, length us, event | category | flops | bytes accessed | tf_op | source)
XLA Modules:
  0.0 224.9 jit_solution(1685540654432374637)
XLA Ops:
  7.2 1.0 copy.10
  9.0 1.1 reduce-window.6
  10.8 2.4 %scatter_custom_fusion = s32[768]{0:T(1024)S(1)} fusion(s32[512]{0:T(512)S(1)} %bitcast.57, s32[512]{0:T(512)S(1)} %iota.15, s32[]{:T(128)} %constant.26.clone.1), kind=kCustom, calls=%fused_computation.57 | custom fusion | bytes 3076 | tf_op jit(solution)/shard_map/scatter | solution.py:39
  14.3 5.0 %gather_fusion.1 = f32[768]{0:T(1024)S(1)} fusion(f32[512]{0:T(512)S(1)} %div.25, s32[1024]{0:T(1024)S(1)} %get-tuple-element.7), kind=kCustom, calls=%fused_computation.1 | custom fusion | bytes 9216 | tf_op jit(solution)/shard_map/gather | solution.py:45
  19.4 3.5 %gather_fusion.2 = bf16[768,1024]{1,0:T(8,128)(2,1)} fusion(bf16[256,1024]{1,0:T(8,128)(2,1)S(1)} %copy-done.2, s32[1024]{0:T(1024)S(1)} %get-tuple-element.8), kind=kCustom, calls=%fused_computation.2 | custom fusion | bytes 3148800 | tf_op jit(solution)/shard_map/gather | solution.py:47
  23.0 2.8 %broadcast_multiply_fusion = bf16[8,96,1024]{2,1,0:T(8,128)(2,1)} fusion(bf16[8,96,1024]{2,1,0:T(8,128)(2,1)} %bitcast.54, bf16[8,96]{1,0:T(8,128)(2,1)S(1)} %reshape.196), kind=kLoop, calls=%fused_computation.32 | loop fusion | flops 786432 | bytes 3147264 | tf_op jit(solution)/shard_map/mul | solution.py:47
  25.8 7.3 %all-to-all-start.1 = ((bf16[8,96,1024]{2,1,0:T(8,128)(2,1)}), bf16[8,96,1024]{2,1,0:T(8,128)(2,1)}, u32[]{:S(2)}, u32[]{:S(2)}) async-start(bf16[8,96,1024]{2,1,0:T(8,128)(2,1)} %broadcast_multiply_fusion), calls=%async_computation.1 | async-start | bytes 3145728 | tf_op jit(solution)/shard_map/all_to_all | solution.py:52
  33.1 4.2 %gather_fusion = bf16[768,2048]{1,0:T(8,128)(2,1)} fusion(bf16[256,2048]{1,0:T(8,128)(2,1)S(1)} %copy-done.1, s32[1024]{0:T(1024)S(1)} %get-tuple-element.8), kind=kCustom, calls=%fused_computation | custom fusion | bytes 6294528 | tf_op jit(solution)/shard_map/gather | solution.py:48
  37.4 4.1 %fusion = bf16[8,96,2048]{2,1,0:T(8,128)(2,1)} fusion(bf16[8,96,2048]{2,1,0:T(8,128)(2,1)} %bitcast.53, f32[8,96]{1,0:T(8,128)S(1)} %mul.111), kind=kLoop, calls=%fused_computation.7 | loop fusion | flops 4718592 | bytes 6294528 | tf_op jit(solution)/shard_map/convert_element_type | solution.py:48
  41.5 28.7 %all-to-all-done.1 = bf16[8,96,1024]{2,1,0:T(8,128)(2,1)} async-done(((bf16[8,96,1024]{2,1,0:T(8,128)(2,1)}), bf16[8,96,1024]{2,1,0:T(8,128)(2,1)}, u32[]{:S(2)}, u32[]{:S(2)}) %all-to-all-start.1) | async-done | bytes 1572896 | tf_op jit(solution)/shard_map/all_to_all | solution.py:52
  70.2 4.4 %all-to-all-start = ((bf16[8,96,2048]{2,1,0:T(8,128)(2,1)}), bf16[8,96,2048]{2,1,0:T(8,128)(2,1)}, u32[]{:S(2)}, u32[]{:S(2)}) async-start(bf16[8,96,2048]{2,1,0:T(8,128)(2,1)} %fusion), calls=%async_computation | async-start | bytes 6291456 | tf_op jit(solution)/shard_map/all_to_all | solution.py:53
  74.9 4.9 %fusion.15 = f32[768,1024]{1,0:T(8,128)} fusion(bf16[768,1024]{1,0:T(8,128)(2,1)} %bitcast.12, bf16[1,1024,1024]{2,1,0:T(8,128)(2,1)S(1)} %copy-done), kind=kOutput, calls=%fused_computation.24 | convolution fusion | flops 1610612736 | bytes 6815744 | tf_op jit(solution)/shard_map/dot_general | solution.py:68
  79.8 65.1 %all-to-all-done = bf16[8,96,2048]{2,1,0:T(8,128)(2,1)} async-done(((bf16[8,96,2048]{2,1,0:T(8,128)(2,1)}), bf16[8,96,2048]{2,1,0:T(8,128)(2,1)}, u32[]{:S(2)}, u32[]{:S(2)}) %all-to-all-start) | async-done | bytes 3145760 | tf_op jit(solution)/shard_map/all_to_all | solution.py:53
  144.8 9.1 %fusion.10 = bf16[768,1024]{1,0:T(8,128)(2,1)S(1)} fusion(f32[768,1024]{1,0:T(8,128)} %fusion.15, bf16[768,2048]{1,0:T(8,128)(2,1)} %bitcast.9, bf16[1,1024,2048]{2,1,0:T(8,128)(2,1)} %param.11), kind=kOutput, calls=%fused_computation.20 | convolution fusion | flops 3236954112 | bytes 12058624 | tf_op jit(solution)/shard_map/dot_general | solution.py:71
  153.9 1.2 copy-done.3
  155.2 3.5 %fusion.17 = f32[1024,768]{0,1:T(8,128)} fusion(bf16[768,1024]{1,0:T(8,128)(2,1)S(1)} %fusion.10, bf16[1,1024,1024]{2,1,0:T(8,128)(2,1)S(1)} %copy-done), kind=kOutput, calls=%fused_computation.26 | convolution fusion | flops 1610612736 | bytes 6815744 | tf_op jit(solution)/shard_map/dot_general | solution.py:76
  158.7 5.0 %fusion.20 = bf16[1,1024,1024]{2,1,0:T(8,128)(2,1)} fusion(bf16[768,1024]{1,0:T(8,128)(2,1)} %bitcast.12, bf16[768,1024]{1,0:T(8,128)(2,1)} %copy-done.3), kind=kOutput, calls=%fused_computation.27 | convolution fusion | flops 1612709888 | bytes 5242880 | tf_op jit(solution)/shard_map/dot_general | solution.py:95
  163.7 31.9 %reduce-scatter.2.cloned.1.call-done = f32[256,768]{0,1:T(8,128)} async-done(((f32[1024,768]{0,1:T(8,128)}), f32[256,768]{0,1:T(8,128)}) %reduce-scatter.2.cloned.1.call-update) | async-done | bytes 786448 | tf_op jit(solution)/shard_map/reduce_scatter | solution.py:75
  195.7 1.9 convert_element_type.61
  197.6 5.5 %all-to-all-start.2 = ((bf16[256,8,96]{0,2,1:T(8,128)(2,1)}), bf16[256,8,96]{0,2,1:T(8,128)(2,1)S(1)}, u32[]{:S(2)}, u32[]{:S(2)}) async-start(bf16[256,8,96]{0,2,1:T(8,128)(2,1)} %bitcast.15), calls=%async_computation.3 | async-start | bytes 786432 | tf_op jit(solution)/shard_map/all_to_all | solution.py:83
  203.1 8.6 %fusion.3 = bf16[1,1024,2048]{2,1,0:T(8,128)(2,1)} fusion(bf16[768,2048]{1,0:T(8,128)(2,1)} %bitcast.9, f32[768,1024]{1,0:T(8,128)} %fusion.15), kind=kOutput, calls=%fused_computation.13 | convolution fusion | flops 3232497664 | bytes 10485760 | tf_op jit(solution)/shard_map/dot_general | solution.py:98
  211.7 2.9 %all-to-all-done.2 = bf16[256,8,96]{0,2,1:T(8,128)(2,1)S(1)} async-done(((bf16[256,8,96]{0,2,1:T(8,128)(2,1)}), bf16[256,8,96]{0,2,1:T(8,128)(2,1)S(1)}, u32[]{:S(2)}, u32[]{:S(2)}) %all-to-all-start.2) | async-done | bytes 393248 | tf_op jit(solution)/shard_map/all_to_all | solution.py:83
  214.6 1.9 gather_fusion.3
  216.7 1.3 reduce.1
  (31 shorter events, 3.0 us)
Async XLA Ops:
  7.2 67.7 %copy-start = (bf16[1,1024,1024]{2,1,0:T(8,128)(2,1)S(1)}, bf16[1,1024,1024]{2,1,0:T(8,128)(2,1)}, u32[]{:S(2)}) copy-start(bf16[1,1024,1024]{2,1,0:T(8,128)(2,1)} %param.10) | copy-start | bytes 6291460
  7.2 12.2 %copy-start.2 = (bf16[256,1024]{1,0:T(8,128)(2,1)S(1)}, bf16[256,1024]{1,0:T(8,128)(2,1)}, u32[]{:S(2)}) copy-start(bf16[256,1024]{1,0:T(8,128)(2,1)} %param.6) | copy-start | bytes 1572868
  23.0 10.2 %copy-start.1 = (bf16[256,2048]{1,0:T(8,128)(2,1)S(1)}, bf16[256,2048]{1,0:T(8,128)(2,1)}, u32[]{:S(2)}) copy-start(bf16[256,2048]{1,0:T(8,128)(2,1)} %param.7) | copy-start | bytes 3145732
  25.8 44.4 %all-to-all-start.1 = ((bf16[8,96,1024]{2,1,0:T(8,128)(2,1)}), bf16[8,96,1024]{2,1,0:T(8,128)(2,1)}, u32[]{:S(2)}, u32[]{:S(2)}) async-start(bf16[8,96,1024]{2,1,0:T(8,128)(2,1)} %broadcast_multiply_fusion), calls=%async_computation.1 | async-start | bytes 3145728 | tf_op jit(solution)/shard_map/all_to_all | solution.py:52
  70.2 74.6 %all-to-all-start = ((bf16[8,96,2048]{2,1,0:T(8,128)(2,1)}), bf16[8,96,2048]{2,1,0:T(8,128)(2,1)}, u32[]{:S(2)}, u32[]{:S(2)}) async-start(bf16[8,96,2048]{2,1,0:T(8,128)(2,1)} %fusion), calls=%async_computation | async-start | bytes 6291456 | tf_op jit(solution)/shard_map/all_to_all | solution.py:53
  74.6 121.0 %reduce-scatter.2.cloned.1.call-start = ((), (), s32[]{:S(2)}) async-start(), calls=%async_computation.4 | async-start | bytes 3932160 | tf_op jit(solution)/shard_map/reduce_scatter | solution.py:75
  153.9 1.2 copy-start.3
  197.6 17.0 %all-to-all-start.2 = ((bf16[256,8,96]{0,2,1:T(8,128)(2,1)}), bf16[256,8,96]{0,2,1:T(8,128)(2,1)S(1)}, u32[]{:S(2)}, u32[]{:S(2)}) async-start(bf16[256,8,96]{0,2,1:T(8,128)(2,1)} %bitcast.15), calls=%async_computation.3 | async-start | bytes 786432 | tf_op jit(solution)/shard_map/all_to_all | solution.py:83
Sparse Core Ops, SparseCore 0:
  158.8 36.8 reduce-scatter.1
where the time goes:
time: 225 us
  waiting for transfers between devices  129 us (57%)
  matrix products  31.2 us (14%)
  local copies, waits for them, and re-layouts  20.6 us (9%)
  starting transfers between devices  17.4 us (8%)
  between operations  14.2 us (6%)
  other arithmetic  12.9 us (6%)
    all_to_all x1, waiting for transfers between devices, shards(): lax.all_to_all(packed_dy, 'ep', split_axis=0, concat_axis=0, tiled=True)  65.1 us
    reduce_scatter x1, waiting for transfers between devices, shards(): lax.psum_scatter(lax.dot_general(weight_in, back_pre, (((1,), (1,)), ((),...  31.9 us
    all_to_all x1, waiting for transfers between devices, shards(): lax.all_to_all(packed_x, 'ep', split_axis=0, concat_axis=0, tiled=True)  28.7 us
    dot_general x1, matrix products, shards(): lax.dot_general(rows_dy, weight_out, (((1,), (1,)), ((), ())), preferred_...  9.11 us
    dot_general x1, matrix products, span_grads(): lax.dot_general(act_cols, rows_dy, (((0,), (0,)), ((), ())), preferred_el...  8.64 us
    all_to_all x1, starting transfers between devices, shards(): lax.all_to_all(packed_x, 'ep', split_axis=0, concat_axis=0, tiled=True)  7.28 us
    all_to_all x1, starting transfers between devices, shards(): lax.all_to_all(summed.astype(jnp.bfloat16), 'ep', split_axis=1, concat_ax...  5.49 us
    dot_general x1, matrix products, span_grads(): lax.dot_general(pre_cols, rows_x, (((0,), (0,)), ((), ())), preferred_ele...  5.04 us
  transfers between devices with their start and end apart: 4, of which 4 were waited for; matrix products, arithmetic and copies ran while one was open for 12% of the time, Pallas kernels for 0%

commit v1 on v0

--- a/solution.py
+++ b/solution.py
@@ -5,6 +5,29 @@
 from jax.sharding import PartitionSpec as P
 
 E = 8
+
+
+def in_blocks(x, dim, size):
+    before, after = (x.shape[:dim], x.shape[dim + 1 :])
+    return jnp.moveaxis(x.reshape(*before, size, -1, *after), dim, 0)
+
+
+def laid_out(pieces, dim):
+    dims = list(pieces.shape[1:])
+    dims[dim] *= pieces.shape[0]
+    return jnp.moveaxis(pieces, 0, dim).reshape(dims)
+
+
+def rotated_exchange(x, axis, split_dim, concat_dim):
+    size, index = (lax.axis_size(axis), lax.axis_index(axis))
+    blocks = in_blocks(x, split_dim, size)
+    out = blocks
+    for hop in range(1, size):
+        target, source = ((index + hop) % size, (index - hop) % size)
+        sent = lax.dynamic_index_in_dim(blocks, target, 0)
+        other = lax.ppermute(sent, axis, [(i, (i + hop) % size) for i in range(size)])
+        out = lax.dynamic_update_slice_in_dim(out, other, source, axis=0)
+    return laid_out(out, concat_dim)
 
 
 def shifted(value, axis, by):
@@ -80,9 +103,7 @@
         scatter_dimension=0,
         tiled=True,
     )
-    returned = lax.all_to_all(
-        summed.astype(jnp.bfloat16), "ep", split_axis=1, concat_axis=1, tiled=True
-    )
+    returned = rotated_exchange(summed.astype(jnp.bfloat16), "ep", 1, 1)
     picked = returned[:, positions].astype(jnp.float32)
     grad_in = jnp.sum(picked.reshape(picked.shape[0], tokens_here, 2), axis=2).T.astype(
         jnp.bfloat16

time: 225 us -> 228 us (1.013)
  starting transfers between devices: 17.4 us -> 24.4 us
  waiting for transfers between devices: 129 us -> 124 us
    ppermute x0 -> x7, starting transfers between devices: none -> 12.4 us  [rotated_exchange(): lax.ppermute(sent, axis, [(i, (i + hop) % size) for i in range(size)])]
    all_to_all x1 -> x0, starting transfers between devices: 5.49 us -> none  [shards(): lax.all_to_all(summed.astype(jnp.bfloat16), 'ep', split_axis=1, concat_ax...]
    reduce_scatter x1, waiting for transfers between devices: 31.9 us -> 28 us  [shards(): lax.psum_scatter(lax.dot_general(weight_in, back_pre, (((1,), (1,)), ((),...]
    all_to_all x1 -> x0, waiting for transfers between devices: 2.92 us -> none  [shards(): lax.all_to_all(summed.astype(jnp.bfloat16), 'ep', split_axis=1, concat_ax...]
    ppermute x0 -> x7, waiting for transfers between devices: none -> 2.54 us  [rotated_exchange(): lax.ppermute(sent, axis, [(i, (i + hop) % size) for i in range(size)])]
  transfers between devices with their start and end apart: 4 -> 10, of which waited for: 4 -> 5; matrix products, arithmetic and copies ran while one was open for 12% -> 12% of each run, Pallas kernels for 0% -> 0%
where the time goes in v1:
time: 228 us; the launch traced here: 227 us
  waiting for transfers between devices  124 us (54%)
  matrix products  31.2 us (14%)
  starting transfers between devices  24.4 us (11%)
  local copies, waits for them, and re-layouts  20.4 us (9%)
  between operations  14.5 us (6%)
  other arithmetic  12.3 us (5%)
    all_to_all x1, waiting for transfers between devices, shards(): lax.all_to_all(packed_dy, 'ep', split_axis=0, concat_axis=0, tiled=True)  65.1 us
    all_to_all x1, waiting for transfers between devices, shards(): lax.all_to_all(packed_x, 'ep', split_axis=0, concat_axis=0, tiled=True)  28.7 us
    reduce_scatter x1, waiting for transfers between devices, shards(): lax.psum_scatter(lax.dot_general(weight_in, back_pre, (((1,), (1,)), ((),...  28 us
    ppermute x7, starting transfers between devices, rotated_exchange(): lax.ppermute(sent, axis, [(i, (i + hop) % size) for i in range(size)])  12.4 us
    dot_general x1, matrix products, shards(): lax.dot_general(rows_dy, weight_out, (((1,), (1,)), ((), ())), preferred_...  9.11 us
    dot_general x1, matrix products, span_grads(): lax.dot_general(act_cols, rows_dy, (((0,), (0,)), ((), ())), preferred_el...  8.64 us
    all_to_all x1, starting transfers between devices, shards(): lax.all_to_all(packed_x, 'ep', split_axis=0, concat_axis=0, tiled=True)  7.28 us
    dot_general x1, matrix products, span_grads(): lax.dot_general(pre_cols, rows_x, (((0,), (0,)), ((), ())), preferred_ele...  5.04 us
  transfers between devices with their start and end apart: 10, of which 5 were waited for; matrix products, arithmetic and copies ran while one was open for 12% of the time, Pallas kernels for 0%

profile of v1, /device:TPU:0, one launch (start us, length us, event | category | flops | bytes accessed | tf_op | source)
XLA Modules:
  0.0 227.1 jit_solution(11038511847428930730)
XLA Ops:
  10.8 2.4 %scatter_custom_fusion = s32[768]{0:T(1024)S(1)} fusion(s32[512]{0:T(512)S(1)} %bitcast.77, s32[512]{0:T(512)S(1)} %iota.15, s32[]{:T(128)} %constant.145.clone.1), kind=kCustom, calls=%fused_computation.71 | custom fusion | bytes 3076 | tf_op jit(solution)/shard_map/scatter | solution.py:62
  14.3 5.0 %gather_fusion.1 = f32[768]{0:T(1024)S(1)} fusion(f32[512]{0:T(512)S(1)} %div.25, s32[1024]{0:T(1024)S(1)} %get-tuple-element.14), kind=kCustom, calls=%fused_computation.1 | custom fusion | bytes 9216 | tf_op jit(solution)/shard_map/gather | solution.py:68
  19.4 3.5 %gather_fusion.2 = bf16[768,1024]{1,0:T(8,128)(2,1)} fusion(bf16[256,1024]{1,0:T(8,128)(2,1)S(1)} %copy-done.2, s32[1024]{0:T(1024)S(1)} %get-tuple-element.15), kind=kCustom, calls=%fused_computation.2 | custom fusion | bytes 3148800 | tf_op jit(solution)/shard_map/gather | solution.py:70
  23.0 2.8 %broadcast_multiply_fusion = bf16[8,96,1024]{2,1,0:T(8,128)(2,1)} fusion(bf16[8,96,1024]{2,1,0:T(8,128)(2,1)} %bitcast.74, bf16[8,96]{1,0:T(8,128)(2,1)S(1)} %reshape.209), kind=kLoop, calls=%fused_computation.32 | loop fusion | flops 786432 | bytes 3147264 | tf_op jit(solution)/shard_map/mul | solution.py:70
  25.8 7.3 %all-to-all-start.1 = ((bf16[8,96,1024]{2,1,0:T(8,128)(2,1)}), bf16[8,96,1024]{2,1,0:T(8,128)(2,1)}, u32[]{:S(2)}, u32[]{:S(2)}) async-start(bf16[8,96,1024]{2,1,0:T(8,128)(2,1)} %broadcast_multiply_fusion), calls=%async_computation.1 | async-start | bytes 3145728 | tf_op jit(solution)/shard_map/all_to_all | solution.py:75
  33.1 4.2 %gather_fusion = bf16[768,2048]{1,0:T(8,128)(2,1)} fusion(bf16[256,2048]{1,0:T(8,128)(2,1)S(1)} %copy-done.1, s32[1024]{0:T(1024)S(1)} %get-tuple-element.15), kind=kCustom, calls=%fused_computation | custom fusion | bytes 6294528 | tf_op jit(solution)/shard_map/gather | solution.py:71
  37.4 4.1 %fusion = bf16[8,96,2048]{2,1,0:T(8,128)(2,1)} fusion(bf16[8,96,2048]{2,1,0:T(8,128)(2,1)} %bitcast.73, f32[8,96]{1,0:T(8,128)S(1)} %mul.111), kind=kLoop, calls=%fused_computation.7 | loop fusion | flops 4718592 | bytes 6294528 | tf_op jit(solution)/shard_map/convert_element_type | solution.py:71
  41.5 28.7 %all-to-all-done.1 = bf16[8,96,1024]{2,1,0:T(8,128)(2,1)} async-done(((bf16[8,96,1024]{2,1,0:T(8,128)(2,1)}), bf16[8,96,1024]{2,1,0:T(8,128)(2,1)}, u32[]{:S(2)}, u32[]{:S(2)}) %all-to-all-start.1) | async-done | bytes 1572896 | tf_op jit(solution)/shard_map/all_to_all | solution.py:75
  70.2 4.5 %all-to-all-start = ((bf16[8,96,2048]{2,1,0:T(8,128)(2,1)}), bf16[8,96,2048]{2,1,0:T(8,128)(2,1)}, u32[]{:S(2)}, u32[]{:S(2)}) async-start(bf16[8,96,2048]{2,1,0:T(8,128)(2,1)} %fusion), calls=%async_computation | async-start | bytes 6291456 | tf_op jit(solution)/shard_map/all_to_all | solution.py:76
  74.9 4.9 %fusion.15 = f32[768,1024]{1,0:T(8,128)} fusion(bf16[768,1024]{1,0:T(8,128)(2,1)} %bitcast.12, bf16[1,1024,1024]{2,1,0:T(8,128)(2,1)S(1)} %copy-done), kind=kOutput, calls=%fused_computation.24 | convolution fusion | flops 1610612736 | bytes 6815744 | tf_op jit(solution)/shard_map/dot_general | solution.py:91
  79.8 65.1 %all-to-all-done = bf16[8,96,2048]{2,1,0:T(8,128)(2,1)} async-done(((bf16[8,96,2048]{2,1,0:T(8,128)(2,1)}), bf16[8,96,2048]{2,1,0:T(8,128)(2,1)}, u32[]{:S(2)}, u32[]{:S(2)}) %all-to-all-start) | async-done | bytes 3145760 | tf_op jit(solution)/shard_map/all_to_all | solution.py:76
  144.8 9.1 %fusion.10 = bf16[768,1024]{1,0:T(8,128)(2,1)S(1)} fusion(f32[768,1024]{1,0:T(8,128)} %fusion.15, bf16[768,2048]{1,0:T(8,128)(2,1)} %bitcast.9, bf16[1,1024,2048]{2,1,0:T(8,128)(2,1)} %param.11), kind=kOutput, calls=%fused_computation.20 | convolution fusion | flops 3236954112 | bytes 12058624 | tf_op jit(solution)/shard_map/dot_general | solution.py:94
  155.1 3.5 %fusion.17 = f32[1024,768]{0,1:T(8,128)} fusion(bf16[768,1024]{1,0:T(8,128)(2,1)S(1)} %fusion.10, bf16[1,1024,1024]{2,1,0:T(8,128)(2,1)S(1)} %copy-done), kind=kOutput, calls=%fused_computation.26 | convolution fusion | flops 1610612736 | bytes 6815744 | tf_op jit(solution)/shard_map/dot_general | solution.py:99
  158.9 8.6 %fusion.3 = bf16[1,1024,2048]{2,1,0:T(8,128)(2,1)} fusion(bf16[768,2048]{1,0:T(8,128)(2,1)} %bitcast.9, f32[768,1024]{1,0:T(8,128)} %fusion.15), kind=kOutput, calls=%fused_computation.13 | convolution fusion | flops 3232497664 | bytes 10485760 | tf_op jit(solution)/shard_map/dot_general | solution.py:119
  167.5 28.0 %reduce-scatter.2.cloned.1.call-done = f32[256,768]{0,1:T(8,128)} async-done(((f32[1024,768]{0,1:T(8,128)}), f32[256,768]{0,1:T(8,128)}) %reduce-scatter.2.cloned.1.call-update) | async-done | bytes 786448 | tf_op jit(solution)/shard_map/reduce_scatter | solution.py:98
  196.8 1.8 collective-permute-start
  198.6 5.0 %fusion.20 = bf16[1,1024,1024]{2,1,0:T(8,128)(2,1)} fusion(bf16[768,1024]{1,0:T(8,128)(2,1)} %bitcast.12, bf16[768,1024]{1,0:T(8,128)(2,1)} %copy-done.3), kind=kOutput, calls=%fused_computation.27 | convolution fusion | flops 1612709888 | bytes 5242880 | tf_op jit(solution)/shard_map/dot_general | solution.py:116
  203.6 1.5 collective-permute-start.1
  205.1 2.4 %collective-permute-start.2 = (bf16[1,256,96]{1,2,0:T(8,128)(2,1)S(1)}, bf16[1,256,96]{1,2,0:T(8,128)(2,1)S(1)}, u32[]{:S(2)}, u32[]{:S(2)}) collective-permute-start(bf16[1,256,96]{1,2,0:T(8,128)(2,1)S(1)} %get-tuple-element.9), channel_id=1, source_target_pairs={{0,12},{4,16},{8,20},{12,24},{16,28},{20,0},{24,4},{28,8},{1,13},{... | collective-permute-start | bytes 147464 | tf_op jit(solution)/shard_map/ppermute | solution.py:28
  208.9 2.4 %collective-permute-start.4 = (bf16[1,256,96]{1,2,0:T(8,128)(2,1)S(1)}, bf16[1,256,96]{1,2,0:T(8,128)(2,1)S(1)}, u32[]{:S(2)}, u32[]{:S(2)}) collective-permute-start(bf16[1,256,96]{1,2,0:T(8,128)(2,1)S(1)} %get-tuple-element.7), channel_id=1, source_target_pairs={{0,20},{4,24},{8,28},{12,0},{16,4},{20,8},{24,12},{28,16},{1,21},{... | collective-permute-start | bytes 147464 | tf_op jit(solution)/shard_map/ppermute | solution.py:28
  211.3 1.4 collective-permute-start.5
  212.8 1.5 collective-permute-start.6
  214.4 1.4 collective-permute-done.5
  216.9 1.9 gather_fusion.3
  (51 shorter events, 11.3 us)
Async XLA Ops:
  7.2 67.7 %copy-start = (bf16[1,1024,1024]{2,1,0:T(8,128)(2,1)S(1)}, bf16[1,1024,1024]{2,1,0:T(8,128)(2,1)}, u32[]{:S(2)}) copy-start(bf16[1,1024,1024]{2,1,0:T(8,128)(2,1)} %param.10) | copy-start | bytes 6291460
  7.2 12.2 %copy-start.2 = (bf16[256,1024]{1,0:T(8,128)(2,1)S(1)}, bf16[256,1024]{1,0:T(8,128)(2,1)}, u32[]{:S(2)}) copy-start(bf16[256,1024]{1,0:T(8,128)(2,1)} %param.6) | copy-start | bytes 1572868
  23.0 10.1 %copy-start.1 = (bf16[256,2048]{1,0:T(8,128)(2,1)S(1)}, bf16[256,2048]{1,0:T(8,128)(2,1)}, u32[]{:S(2)}) copy-start(bf16[256,2048]{1,0:T(8,128)(2,1)} %param.7) | copy-start | bytes 3145732
  25.8 44.4 %all-to-all-start.1 = ((bf16[8,96,1024]{2,1,0:T(8,128)(2,1)}), bf16[8,96,1024]{2,1,0:T(8,128)(2,1)}, u32[]{:S(2)}, u32[]{:S(2)}) async-start(bf16[8,96,1024]{2,1,0:T(8,128)(2,1)} %broadcast_multiply_fusion), calls=%async_computation.1 | async-start | bytes 3145728 | tf_op jit(solution)/shard_map/all_to_all | solution.py:75
  70.2 74.6 %all-to-all-start = ((bf16[8,96,2048]{2,1,0:T(8,128)(2,1)}), bf16[8,96,2048]{2,1,0:T(8,128)(2,1)}, u32[]{:S(2)}, u32[]{:S(2)}) async-start(bf16[8,96,2048]{2,1,0:T(8,128)(2,1)} %fusion), calls=%async_computation | async-start | bytes 6291456 | tf_op jit(solution)/shard_map/all_to_all | solution.py:76
  74.6 120.9 %reduce-scatter.2.cloned.1.call-start = ((), (), s32[]{:S(2)}) async-start(), calls=%async_computation.3 | async-start | bytes 3932160 | tf_op jit(solution)/shard_map/reduce_scatter | solution.py:98
  153.9 1.1 copy-start.3
  196.8 14.5 %collective-permute-start = (bf16[1,256,96]{1,2,0:T(8,128)(2,1)S(1)}, bf16[1,256,96]{1,2,0:T(8,128)(2,1)S(1)}, u32[]{:S(2)}, u32[]{:S(2)}) collective-permute-start(bf16[1,256,96]{1,2,0:T(8,128)(2,1)S(1)} %get-tuple-element.11), channel_id=1, source_target_pairs={{0,4},{4,8},{8,12},{12,16},{16,20},{20,24},{24,28},{28,0},{1,5},{5... | collective-permute-start | bytes 147464 | tf_op jit(solution)/shard_map/ppermute | solution.py:28
  203.6 9.2 %collective-permute-start.1 = (bf16[1,256,96]{1,2,0:T(8,128)(2,1)S(1)}, bf16[1,256,96]{1,2,0:T(8,128)(2,1)S(1)}, u32[]{:S(2)}, u32[]{:S(2)}) collective-permute-start(bf16[1,256,96]{1,2,0:T(8,128)(2,1)S(1)} %get-tuple-element.10), channel_id=1, source_target_pairs={{0,8},{4,12},{8,16},{12,20},{16,24},{20,28},{24,0},{28,4},{1,9},{5... | collective-permute-start | bytes 147464 | tf_op jit(solution)/shard_map/ppermute | solution.py:28
  205.1 9.2 %collective-permute-start.2 = (bf16[1,256,96]{1,2,0:T(8,128)(2,1)S(1)}, bf16[1,256,96]{1,2,0:T(8,128)(2,1)S(1)}, u32[]{:S(2)}, u32[]{:S(2)}) collective-permute-start(bf16[1,256,96]{1,2,0:T(8,128)(2,1)S(1)} %get-tuple-element.9), channel_id=1, source_target_pairs={{0,12},{4,16},{8,20},{12,24},{16,28},{20,0},{24,4},{28,8},{1,13},{... | collective-permute-start | bytes 147464 | tf_op jit(solution)/shard_map/ppermute | solution.py:28
  207.5 6.8 %collective-permute-start.3 = (bf16[1,256,96]{1,2,0:T(8,128)(2,1)S(1)}, bf16[1,256,96]{1,2,0:T(8,128)(2,1)S(1)}, u32[]{:S(2)}, u32[]{:S(2)}) collective-permute-start(bf16[1,256,96]{1,2,0:T(8,128)(2,1)S(1)} %get-tuple-element.8), channel_id=1, source_target_pairs={{0,16},{4,20},{8,24},{12,28},{16,0},{20,4},{24,8},{28,12},{1,17},{... | collective-permute-start | bytes 147464 | tf_op jit(solution)/shard_map/ppermute | solution.py:28
  208.9 5.5 %collective-permute-start.4 = (bf16[1,256,96]{1,2,0:T(8,128)(2,1)S(1)}, bf16[1,256,96]{1,2,0:T(8,128)(2,1)S(1)}, u32[]{:S(2)}, u32[]{:S(2)}) collective-permute-start(bf16[1,256,96]{1,2,0:T(8,128)(2,1)S(1)} %get-tuple-element.7), channel_id=1, source_target_pairs={{0,20},{4,24},{8,28},{12,0},{16,4},{20,8},{24,12},{28,16},{1,21},{... | collective-permute-start | bytes 147464 | tf_op jit(solution)/shard_map/ppermute | solution.py:28
  211.3 4.5 %collective-permute-start.5 = (bf16[1,256,96]{1,2,0:T(8,128)(2,1)S(1)}, bf16[1,256,96]{1,2,0:T(8,128)(2,1)S(1)}, u32[]{:S(2)}, u32[]{:S(2)}) collective-permute-start(bf16[1,256,96]{1,2,0:T(8,128)(2,1)S(1)} %get-tuple-element.6), channel_id=1, source_target_pairs={{0,24},{4,28},{8,0},{12,4},{16,8},{20,12},{24,16},{28,20},{1,25},{... | collective-permute-start | bytes 147464 | tf_op jit(solution)/shard_map/ppermute | solution.py:28
  212.8 4.1 %collective-permute-start.6 = (bf16[1,256,96]{1,2,0:T(8,128)(2,1)S(1)}, bf16[1,256,96]{1,2,0:T(8,128)(2,1)S(1)}, u32[]{:S(2)}, u32[]{:S(2)}) collective-permute-start(bf16[1,256,96]{1,2,0:T(8,128)(2,1)S(1)} %get-tuple-element.5), channel_id=1, source_target_pairs={{0,28},{4,0},{8,4},{12,8},{16,12},{20,16},{24,20},{28,24},{1,29},{... | collective-permute-start | bytes 147464 | tf_op jit(solution)/shard_map/ppermute | solution.py:28
Sparse Core Ops, SparseCore 0:
  158.7 36.7 reduce-scatter.1
